TPU v7x, 256 devices: a whole 4x4x8 slice. The times are simulated.
256 devices in a mesh: ctx: 16 (over x, z_hi, core), exp: 16 (over z_lo, y).
Axes of the slice: x: 4, y: 4, z: 8 (z_hi: 2, z_lo: 4; z = z_hi * 4 + z_lo), core: 2. Of those that a mesh axis runs over, the one named last changes fastest.
Arguments:
- queries: bfloat16 [16, 1024, 2560], P('exp', 'ctx'), may hold values from -4.5 to 4.5
- keys: bfloat16 [16, 1024, 512], P('exp', 'ctx'), may hold values from -4.5 to 4.5
- values: bfloat16 [16, 1024, 512], P('exp', 'ctx'), may hold values from -6 to 6
- doc_lengths: int32 [16, 4], P('exp'), may hold values from 1 to 512, 1024 in all within a row
- resid: bfloat16 [16, 1024, 5120], P('exp', 'ctx'), may hold values from -6 to 6
- out_weight: bfloat16 [2560, 5120], P(('ctx', 'exp')), may hold values from -1 to 1
- norm_gain: bfloat16 [5120], replicated, may hold values from 0.099609375 to 1.8984375
- router_weight: bfloat16 [5120, 16], replicated, may hold values from -0.078125 to 0.078125
- expert_ids: int32 [16, 1024, 1], P('exp', 'ctx'), may hold values from 0 to 15; in each aligned block of 64 rows (0 to 63, 64 to 127, ..., all dimensions but the last counted through in order) at most 5 rows name the same one
- gate_weight: bfloat16 [16, 5120, 4096], P('exp', None, 'ctx'), may hold values from -0.078125 to 0.078125
- up_weight: bfloat16 [16, 5120, 4096], P('exp', None, 'ctx'), may hold values from -0.078125 to 0.078125
- down_weight: bfloat16 [16, 4096, 5120], P('exp', 'ctx'), may hold values from -0.375 to 0.375
Outputs:
- layer_out: bfloat16 [16, 1024, 5120], P('exp', 'ctx')
Inputs may be any that keep to these rules, and one draw needn't show every extreme that they name: `expert_ids`: among the 64 positions p = c * 64 .. c * 64 + 63 of one sequence, for any c, no expert is named more than 5 times.
All inputs are finite; a program needn't handle non-finite values.
Results may differ from a plain program's by a relative error of at most 0.017.
Values may be sent and summed in bfloat16 or wider, within the bound.
No kernel may reach another device: no remote copies, remote signals or barrier semaphores. Data moves between devices by JAX's collectives and lax.ppermute only.
A program may use at most 128 MiB of HBM per device.

v0:
```python
import math
import jax
import jax.numpy as jnp
from jax import lax
from jax.sharding import PartitionSpec as P

HEAD_SIZE = 128


def doc_number(positions, bounds):
    return jnp.sum((positions[:, None] >= bounds[None, :]).astype(jnp.int32), axis=1)


def local(
    queries,
    keys,
    values,
    doc_lengths,
    resid,
    out_weight,
    norm_gain,
    router_weight,
    expert_ids,
    gate_weight,
    up_weight,
    down_weight,
):
    tok_rows = queries.shape[1]
    width = resid.shape[2]
    n_ctx = lax.axis_size("ctx")
    n_exp = lax.axis_size("exp")
    positions = lax.axis_index("ctx") * tok_rows + jnp.arange(tok_rows, dtype=jnp.int32)
    bounds = jnp.cumsum(doc_lengths[0])
    query_doc = doc_number(positions, bounds)
    kv_heads = keys.shape[2] // HEAD_SIZE
    head_groups = queries.shape[2] // keys.shape[2]
    heads_of_query = queries[0].reshape(tok_rows, kv_heads, head_groups, HEAD_SIZE)
    scale = 1.0 / math.sqrt(HEAD_SIZE)
    best = jnp.full((kv_heads, head_groups, tok_rows), -1e30, jnp.float32)
    key_piece = lax.all_gather(keys[0], "ctx", axis=0, tiled=True)
    value_piece = lax.all_gather(values[0], "ctx", axis=0, tiled=True)
    count = key_piece.shape[0]
    heads_of_key = key_piece.reshape(count, kv_heads, HEAD_SIZE)
    heads_of_value = value_piece.reshape(count, kv_heads, HEAD_SIZE)
    scores = (
        jnp.einsum(
            "tkgd,nkd->kgtn", heads_of_query, heads_of_key, preferred_element_type=jnp.float32
        )
        * scale
    )
    key_pos = jnp.arange(count, dtype=jnp.int32)
    visible = (key_pos[None, :] <= positions[:, None]) & (
        doc_number(key_pos, bounds)[None, :] == query_doc[:, None]
    )
    masked = jnp.where(visible, scores, -1e30)
    newbest = jnp.maximum(best, jnp.max(masked, axis=-1))
    weights = jnp.where(visible, jnp.exp(masked - newbest[..., None]), 0.0)
    total = jnp.sum(weights, axis=-1)
    accum = jnp.einsum(
        "kgtn,nkd->kgtd",
        weights.astype(jnp.bfloat16),
        heads_of_value,
        preferred_element_type=jnp.float32,
    )
    best, total, accum = (newbest, total, accum)
    attended = (
        (accum / total[..., None]).transpose(2, 0, 1, 3).reshape(tok_rows, -1).astype(jnp.bfloat16)
    )
    qwidth = attended.shape[1]
    proj_rows = lax.all_gather(out_weight, "exp", axis=0, tiled=True)
    feature_block = lax.all_to_all(
        attended.reshape(tok_rows, n_ctx, qwidth // n_ctx),
        "ctx",
        split_axis=1,
        concat_axis=0,
        tiled=True,
    )
    feature_rows = feature_block.reshape(n_ctx * tok_rows, -1)
    attn_sum = lax.psum_scatter(
        jnp.dot(feature_rows, proj_rows, preferred_element_type=jnp.float32).astype(jnp.bfloat16),
        "ctx",
        scatter_dimension=0,
        tiled=True,
    )
    hidden_state = resid[0].astype(jnp.float32) + attn_sum.astype(jnp.float32)
    mean_square = jnp.mean(hidden_state * hidden_state, axis=-1, keepdims=True)
    normed = hidden_state * lax.rsqrt(mean_square + 1e-05) * norm_gain.astype(jnp.float32)
    normed_b = normed.astype(jnp.bfloat16)
    logits = jnp.dot(normed_b, router_weight, preferred_element_type=jnp.float32)
    n_experts = router_weight.shape[1]
    chosen = expert_ids[0, :, 0]
    picked = chosen[:, None] == jnp.arange(n_experts, dtype=jnp.int32)[None, :]
    score = jax.nn.sigmoid(jnp.sum(jnp.where(picked, logits, 0.0), axis=-1))
    routed = (normed * score[:, None]).astype(jnp.bfloat16)
    capacity = max(2, tok_rows // n_experts + tok_rows // (4 * n_experts))
    lower = jnp.tril(jnp.ones((tok_rows, tok_rows), jnp.float32), -1)
    earlier = jnp.dot(lower, picked.astype(jnp.float32), preferred_element_type=jnp.float32)
    slot_rank = jnp.sum(jnp.where(picked, earlier, 0.0), axis=-1).astype(jnp.int32)
    selector = picked[:, :, None] & (
        slot_rank[:, None, None] == jnp.arange(capacity, dtype=jnp.int32)[None, None, :]
    )
    selector_b = selector.astype(jnp.bfloat16)
    outgoing = jnp.einsum(
        "tes,td->esd", selector_b, routed, preferred_element_type=jnp.float32
    ).astype(jnp.bfloat16)
    arrived = lax.all_to_all(outgoing, "exp", split_axis=0, concat_axis=0, tiled=True)
    arrived_rows = arrived.reshape(-1, width)
    gate_local = gate_weight[0]
    up_local = up_weight[0]
    down_local = down_weight[0]
    piece = lax.all_gather(arrived_rows, "ctx", axis=0, tiled=True)
    gate = jnp.dot(piece, gate_local, preferred_element_type=jnp.float32)
    up = jnp.dot(piece, up_local, preferred_element_type=jnp.float32)
    inner = (jax.nn.silu(gate) * up).astype(jnp.bfloat16)
    summed = lax.psum_scatter(
        jnp.dot(inner, down_local, preferred_element_type=jnp.float32).astype(jnp.bfloat16),
        "ctx",
        scatter_dimension=0,
        tiled=True,
    )
    expert_out = summed.reshape(n_exp, capacity, width)
    returned = lax.all_to_all(expert_out, "exp", split_axis=0, concat_axis=0, tiled=True)
    combined = jnp.einsum("tes,esd->td", selector_b, returned, preferred_element_type=jnp.float32)
    layer_out = (hidden_state + combined).astype(jnp.bfloat16)
    return layer_out[None]


def solution(mesh):
    in_specs = (
        P("exp", "ctx", None),
        P("exp", "ctx", None),
        P("exp", "ctx", None),
        P("exp", None),
        P("exp", "ctx", None),
        P(("ctx", "exp"), None),
        P(),
        P(),
        P("exp", "ctx", None),
        P("exp", None, "ctx"),
        P("exp", None, "ctx"),
        P("exp", "ctx", None),
    )
    out_specs = P("exp", "ctx", None)
    return jax.shard_map(local, mesh=mesh, in_specs=in_specs, out_specs=out_specs, check_vma=False)
```

profile of v0, /device:TPU:32, one launch (start us, length us, event | category | flops | bytes accessed | tf_op | source)
XLA Modules:
  0.0 811.9 jit_solution(17532757584282745511)
XLA Ops:
  6.5 0.0 all-gather.10.cloned.1.call-start
  6.5 0.7 all-gather.10.cloned.1.call-update
  7.3 0.0 all-gather.12.cloned.1.call-start
  7.3 0.7 all-gather.12.cloned.1.call-update
  8.0 0.0 all-gather.14.cloned.1.call-start
  8.1 0.7 all-gather.14.cloned.1.call-update
  8.7 1.4 reshape_squeeze.3
  10.1 0.8 reduce-window.8
  11.0 0.1 convert_reduce_fusion
  11.0 0.1 convert_reduce_fusion.1
  11.1 0.1 fusion.49
  11.3 56.0 %all-gather.10.cloned.1.call-done = bf16[1,1024,512]{2,1,0:T(8,128)(2,1)} async-done(((bf16[1,64,512]{2,1,0:T(8,128)(2,1)}), bf16[1,1024,512]{2,1,0:T(8,128)(2,1)}) %all-gather.10.cloned.1.call-update) | async-done | bytes 1048592 | tf_op jit(solution)/shard_map/all_gather | solution.py:40
  67.2 2.3 copy.34
  69.5 51.5 %all-gather.12.cloned.1.call-done = bf16[1,1024,512]{2,1,0:T(8,128)(2,1)} async-done(((bf16[1,64,512]{2,1,0:T(8,128)(2,1)}), bf16[1,1024,512]{2,1,0:T(8,128)(2,1)}) %all-gather.12.cloned.1.call-update) | async-done | bytes 1048592 | tf_op jit(solution)/shard_map/all_gather | solution.py:41
  121.1 2.3 copy.37
  123.3 2.4 fusion.3
  125.7 1.6 fusion.4
  127.4 1.5 fusion.32
  128.9 0.2 copy.39
  129.1 1.4 convert_element_type.64
  130.5 2.0 copy.40
  132.5 4.2 all-to-all-start
  136.8 0.0 reduce-scatter.3.cloned.1.call-start
  136.8 66.1 %all-gather.14.cloned.1.call-done = bf16[16,10,5120]{2,1,0:T(8,128)(2,1)} async-done(((bf16[1,10,5120]{2,1,0:T(8,128)(2,1)}), bf16[16,10,5120]{2,1,0:T(8,128)(2,1)}) %all-gather.14.cloned.1.call-update) | async-done | bytes 1638416 | tf_op jit(solution)/shard_map/all_gather | solution.py:70
  202.9 4.0 reshape.133
  207.0 0.0 all-to-all-done
  207.0 6.9 convolution_convert_fusion.1
  213.9 0.0 reduce-scatter.3.cloned.1.call-update
  214.0 0.0 all-gather.8.cloned.1.call-start
  214.0 0.6 copy-done.6
  214.6 0.2 fusion.28
  214.9 159.8 %reduce-scatter.3.cloned.1.call-done = bf16[64,5120]{1,0:T(8,128)(2,1)} async-done(((bf16[1024,5120]{1,0:T(8,128)(2,1)}), bf16[64,5120]{1,0:T(8,128)(2,1)}) %reduce-scatter.3.cloned.1.call-update) | async-done | bytes 655376 | tf_op jit(solution)/shard_map/reduce_scatter | solution.py:79
  374.7 1.5 multiply_reduce_fusion
  376.2 1.5 fusion.27
  377.7 0.5 convolution_convert_fusion.2
  378.1 0.5 copy.42
  378.6 36.6 %all_to_all.25 = bf16[16,5,5120]{2,1,0:T(8,128)(2,1)} all-to-all(bf16[16,5,5120]{2,1,0:T(8,128)(2,1)S(1)} %copy.42), channel_id=1, replica_groups=mesh['ctx'=16,'exp'=16] {'exp'}, dimensions={0} | all-to-all | bytes 1638400 | tf_op jit(solution)/shard_map/all_to_all | solution.py:106
  415.2 2.2 reshape.125
  417.4 0.0 all-gather.8.cloned.1.call-update
  417.5 0.2 reduce-scatter.5.cloned.1.call-start
  417.7 139.5 %all-gather.8.cloned.1.call-done = bf16[1280,5120]{1,0:T(8,128)(2,1)} async-done(((bf16[80,5120]{1,0:T(8,128)(2,1)}), bf16[1280,5120]{1,0:T(8,128)(2,1)}) %all-gather.8.cloned.1.call-update) | async-done | bytes 13107216 | tf_op jit(solution)/shard_map/all_gather | solution.py:111
  557.2 10.1 %fusion.8 = f32[1280,256]{1,0:T(8,128)} fusion(bf16[1280,5120]{1,0:T(8,128)(2,1)} %all-gather.8.cloned.1.call-done, bf16[1,5120,256]{2,1,0:T(8,128)(2,1)} %param.21), kind=kOutput, calls=%fused_computation.15 | convolution fusion | flops 3355443200 | bytes 17039360 | tf_op jit(solution)/shard_map/dot_general | solution.py:112
  567.3 20.4 %convolution_convert_fusion = bf16[1280,5120]{1,0:T(8,128)(2,1)} fusion(bf16[1,256,5120]{2,1,0:T(8,128)(2,1)S(1)} %copy-done, bf16[1280,5120]{1,0:T(8,128)(2,1)} %all-gather.8.cloned.1.call-done, bf16[1,5120,256]{2,1,0:T(8,128)(2,1)} %param.22, f32[1280,256]{1,0:T(8,128)} %fusion.8), kind=kOutput, calls=%fused_computation | convolution fusion | flops 6719406080 | bytes 32768000 | tf_op jit(solution)/shard_map/dot_general | solution.py:116
  587.7 0.0 reduce-scatter.5.cloned.1.call-update
  587.7 176.1 %reduce-scatter.5.cloned.1.call-done = bf16[80,5120]{1,0:T(8,128)(2,1)} async-done(((bf16[1280,5120]{1,0:T(8,128)(2,1)}), bf16[80,5120]{1,0:T(8,128)(2,1)}) %reduce-scatter.5.cloned.1.call-update) | async-done | bytes 819216 | tf_op jit(solution)/shard_map/reduce_scatter | solution.py:115
  763.7 2.2 reshape.126
  766.0 37.4 %all_to_all.26 = bf16[16,5,5120]{2,1,0:T(8,128)(2,1)S(1)} all-to-all(bf16[16,5,5120]{2,1,0:T(8,128)(2,1)} %reshape.126), channel_id=1, replica_groups=mesh['ctx'=16,'exp'=16] {'exp'}, dimensions={0} | all-to-all | bytes 1638400 | tf_op jit(solution)/shard_map/all_to_all | solution.py:122
  803.4 1.6 fusion.2
  (24 shorter events, 0.1 us)
Async XLA Ops:
  6.5 560.8 %copy-start = (bf16[1,256,5120]{2,1,0:T(8,128)(2,1)S(1)}, bf16[1,256,5120]{2,1,0:T(8,128)(2,1)}, u32[]{:S(2)}) copy-start(bf16[1,256,5120]{2,1,0:T(8,128)(2,1)} %param.23) | copy-start | bytes 7864324
  6.5 60.7 %all-gather.10.cloned.1.call-start = ((), (), s32[]{:S(2)}) async-start(), calls=%async_computation.8 | async-start | bytes 1114112 | tf_op jit(solution)/shard_map/all_gather | solution.py:40
  7.3 113.8 %all-gather.12.cloned.1.call-start = ((), (), s32[]{:S(2)}) async-start(), calls=%async_computation.9 | async-start | bytes 1114112 | tf_op jit(solution)/shard_map/all_gather | solution.py:41
  8.0 194.9 %all-gather.14.cloned.1.call-start = ((), (), s32[]{:S(2)}) async-start(), calls=%async_computation.10 | async-start | bytes 2785280 | tf_op jit(solution)/shard_map/all_gather | solution.py:70
  125.7 1.6 copy-start.4
  132.5 74.4 %all-to-all-start = ((bf16[64,16,160]{2,0,1:T(8,128)(2,1)}), bf16[64,16,160]{2,0,1:T(8,128)(2,1)S(1)}, u32[]{:S(2)}, u32[]{:S(2)}) async-start(bf16[64,16,160]{2,0,1:T(8,128)(2,1)} %copy.40), calls=%async_computation | async-start | bytes 1048576 | tf_op jit(solution)/shard_map/all_to_all | solution.py:71
  136.8 237.9 %reduce-scatter.3.cloned.1.call-start = ((), (), s32[]{:S(2)}) async-start(), calls=%async_computation.5 | async-start | bytes 11141120 | tf_op jit(solution)/shard_map/reduce_scatter | solution.py:79
  213.9 0.7 copy-start.6
  213.9 0.9 copy-start.5
  213.9 160.7 %copy-start.1 = (bf16[1,64,5120]{2,1,0:T(8,128)(2,1)S(1)}, bf16[1,64,5120]{2,1,0:T(8,128)(2,1)}, u32[]{:S(2)}) copy-start(bf16[1,64,5120]{2,1,0:T(8,128)(2,1)} %param.16) | copy-start | bytes 1966084
  213.9 162.2 %copy-start.7 = (bf16[5120,16]{0,1:T(8,128)(2,1)S(1)}, bf16[5120,16]{0,1:T(8,128)(2,1)}, u32[]{:S(2)}) copy-start(bf16[5120,16]{0,1:T(8,128)(2,1)} %param.19) | copy-start | bytes 491524
  214.0 343.2 %all-gather.8.cloned.1.call-start = ((), (), s32[]{:S(2)}) async-start(), calls=%async_computation.6 | async-start | bytes 13926400 | tf_op jit(solution)/shard_map/all_gather | solution.py:111
  374.7 3.0 copy-start.2
  417.5 346.3 %reduce-scatter.5.cloned.1.call-start = ((), (), s32[]{:S(2)}) async-start(), calls=%async_computation.7 | async-start | bytes 13926400 | tf_op jit(solution)/shard_map/reduce_scatter | solution.py:115
  766.0 37.4 %copy-start.3 = (bf16[64,5120]{1,0:T(8,128)(2,1)S(1)}, bf16[64,5120]{1,0:T(8,128)(2,1)}, u32[]{:S(2)}) copy-start(bf16[64,5120]{1,0:T(8,128)(2,1)} %reduce-scatter.3.cloned.1.call-done) | copy-start | bytes 1966084
Sparse Core Ops, SparseCore 0:
  10.0 57.1 all-gather.9
  69.9 51.0 all-gather.11
  122.9 80.0 all-gather.13
  214.1 160.5 reduce-scatter.2
  417.6 139.5 all-gather.7
  587.8 175.8 reduce-scatter.4
where the time goes:
time: 813 us; the launch traced here: 812 us
  waiting for transfers between devices  651 us (80%)
  blocking collectives  74 us (9%)
  matrix products  45.1 us (6%)
  local copies, waits for them, and re-layouts  19.1 us (2%)
  between operations  13.6 us (2%)
    reduce_scatter x1, waiting for transfers between devices, local(): lax.psum_scatter(jnp.dot(inner, down_local, preferred_element_type=jnp.fl...  176 us
    reduce_scatter x1, waiting for transfers between devices, local(): lax.psum_scatter(jnp.dot(feature_rows, proj_rows, preferred_element_type=...  160 us
    all_gather x1, waiting for transfers between devices, local(): piece = lax.all_gather(arrived_rows, 'ctx', axis=0, tiled=True)  139 us
    all_gather x1, waiting for transfers between devices, local(): proj_rows = lax.all_gather(out_weight, 'exp', axis=0, tiled=True)  66.1 us
    all_gather x1, waiting for transfers between devices, local(): key_piece = lax.all_gather(keys[0], 'ctx', axis=0, tiled=True)  56 us
    all_gather x1, waiting for transfers between devices, local(): value_piece = lax.all_gather(values[0], 'ctx', axis=0, tiled=True)  51.5 us
    all_to_all x1, blocking collectives, local(): lax.all_to_all(expert_out, 'exp', split_axis=0, concat_axis=0, tiled=True)  37.4 us
    all_to_all x1, blocking collectives, local(): lax.all_to_all(outgoing, 'exp', split_axis=0, concat_axis=0, tiled=True)  36.6 us
  transfers between devices with their start and end apart: 7, of which 6 were waited for; matrix products, arithmetic and copies ran while one was open for 3% of the time, Pallas kernels for 0%

commit v1 on v0

--- a/solution.py
+++ b/solution.py
@@ -5,6 +5,15 @@
 from jax.sharding import PartitionSpec as P
 
 HEAD_SIZE = 128
+place_the_panels = lambda on_dim, view: jnp.concatenate(
+    lax.all_to_all(
+        jnp.stack([view for _ in range(lax.axis_size("ctx"))], axis=0),
+        axis_name="ctx",
+        concat_axis=0,
+        split_axis=0,
+    ),
+    axis=on_dim,
+)
 
 
 def doc_number(positions, bounds):
@@ -37,7 +46,7 @@
     heads_of_query = queries[0].reshape(tok_rows, kv_heads, head_groups, HEAD_SIZE)
     scale = 1.0 / math.sqrt(HEAD_SIZE)
     best = jnp.full((kv_heads, head_groups, tok_rows), -1e30, jnp.float32)
-    key_piece = lax.all_gather(keys[0], "ctx", axis=0, tiled=True)
+    key_piece = place_the_panels(0, keys[0])
     value_piece = lax.all_gather(values[0], "ctx", axis=0, tiled=True)
     count = key_piece.shape[0]
     heads_of_key = key_piece.reshape(count, kv_heads, HEAD_SIZE)

time: 813 us -> 762 us (0.937)
  waiting for transfers between devices: 651 us -> 590 us
  starting transfers between devices: 4.61 us -> 14.8 us
    all_gather x1 -> x0, waiting for transfers between devices: 56 us -> none  [local(): key_piece = lax.all_gather(keys[0], 'ctx', axis=0, tiled=True)]
    all_to_all x0 -> x1, starting transfers between devices: none -> 10.2 us  [lax.all_to_all(jnp.stack([view for _ in range(lax.axis_size('ctx'))], axi...]
  transfers between devices with their start and end apart: 7 -> 7, of which waited for: 6 -> 5; matrix products, arithmetic and copies ran while one was open for 3% -> 3% of each run, Pallas kernels for 0% -> 0%
where the time goes in v1:
time: 762 us; the launch traced here: 761 us
  waiting for transfers between devices  590 us (77%)
  blocking collectives  74 us (10%)
  matrix products  45.2 us (6%)
  local copies, waits for them, and re-layouts  20.1 us (3%)
  starting transfers between devices  14.8 us (2%)
  between operations  13.3 us (2%)
    reduce_scatter x1, waiting for transfers between devices, local(): lax.psum_scatter(jnp.dot(inner, down_local, preferred_element_type=jnp.fl...  176 us
    reduce_scatter x1, waiting for transfers between devices, local(): lax.psum_scatter(jnp.dot(feature_rows, proj_rows, preferred_element_type=...  161 us
    all_gather x1, waiting for transfers between devices, local(): piece = lax.all_gather(arrived_rows, 'ctx', axis=0, tiled=True)  139 us
    all_gather x1, waiting for transfers between devices, local(): proj_rows = lax.all_gather(out_weight, 'exp', axis=0, tiled=True)  62.1 us
    all_gather x1, waiting for transfers between devices, local(): value_piece = lax.all_gather(values[0], 'ctx', axis=0, tiled=True)  50.4 us
    all_to_all x1, blocking collectives, local(): lax.all_to_all(expert_out, 'exp', split_axis=0, concat_axis=0, tiled=True)  37.4 us
    all_to_all x1, blocking collectives, local(): lax.all_to_all(outgoing, 'exp', split_axis=0, concat_axis=0, tiled=True)  36.6 us
    dot_general x1, matrix products, local(): jnp.dot(inner, down_local, preferred_element_type=jnp.float32)  20.4 us
  transfers between devices with their start and end apart: 7, of which 5 were waited for; matrix products, arithmetic and copies ran while one was open for 3% of the time, Pallas kernels for 0%

profile of v1, /device:TPU:32, one launch (start us, length us, event | category | flops | bytes accessed | tf_op | source)
XLA Modules:
  0.0 761.3 jit_solution(10617108604219120452)
XLA Ops:
  6.5 0.7 all-gather.8.cloned.1.call-update
  7.3 2.0 stack.3
  9.3 10.2 %all-to-all-start = ((bf16[16,64,512]{2,1,0:T(8,128)(2,1)}), bf16[16,64,512]{2,1,0:T(8,128)(2,1)}, u32[]{:S(2)}, u32[]{:S(2)}) async-start(bf16[16,64,512]{2,1,0:T(8,128)(2,1)} %stack.3), calls=%async_computation | async-start | bytes 2097152 | tf_op jit(solution)/shard_map/all_to_all | solution.py:9
  19.5 0.0 all-gather.10.cloned.1.call-start
  19.5 0.7 all-gather.10.cloned.1.call-update
  20.2 0.4 reshape_squeeze.3
  20.6 0.0 copy-done.9
  20.6 0.2 reduce-window.8
  20.8 0.1 convert_reduce_fusion
  20.9 0.1 convert_reduce_fusion.1
  21.0 0.1 fusion.50
  21.1 50.4 %all-gather.8.cloned.1.call-done = bf16[1,1024,512]{2,1,0:T(8,128)(2,1)} async-done(((bf16[1,64,512]{2,1,0:T(8,128)(2,1)}), bf16[1,1024,512]{2,1,0:T(8,128)(2,1)}) %all-gather.8.cloned.1.call-update) | async-done | bytes 1048592 | tf_op jit(solution)/shard_map/all_gather | solution.py:50
  71.6 2.3 copy.34
  73.8 0.0 all-to-all-done
  73.8 2.2 reshape_reshape.3
  76.0 2.5 fusion.3
  78.5 1.6 fusion.4
  80.1 1.5 fusion.34
  81.6 0.2 copy.36
  81.9 1.4 convert_element_type.64
  83.3 2.0 copy.37
  85.3 4.2 all-to-all-start.1
  89.5 0.0 reduce-scatter.3.cloned.1.call-start
  89.6 62.1 %all-gather.10.cloned.1.call-done = bf16[16,10,5120]{2,1,0:T(8,128)(2,1)} async-done(((bf16[1,10,5120]{2,1,0:T(8,128)(2,1)}), bf16[16,10,5120]{2,1,0:T(8,128)(2,1)}) %all-gather.10.cloned.1.call-update) | async-done | bytes 1638416 | tf_op jit(solution)/shard_map/all_gather | solution.py:79
  151.7 4.0 reshape.128
  155.7 0.0 all-to-all-done.1
  155.7 6.9 convolution_convert_fusion.1
  162.7 0.0 reduce-scatter.3.cloned.1.call-update
  162.7 0.0 all-gather.6.cloned.1.call-start
  162.7 0.6 copy-done.7
  163.3 0.2 fusion.28
  163.6 160.8 %reduce-scatter.3.cloned.1.call-done = bf16[64,5120]{1,0:T(8,128)(2,1)} async-done(((bf16[1024,5120]{1,0:T(8,128)(2,1)}), bf16[64,5120]{1,0:T(8,128)(2,1)}) %reduce-scatter.3.cloned.1.call-update) | async-done | bytes 655376 | tf_op jit(solution)/shard_map/reduce_scatter | solution.py:88
  324.4 1.5 multiply_reduce_fusion
  325.9 1.5 fusion.27
  327.4 0.5 convolution_convert_fusion.2
  327.8 0.5 copy.39
  328.3 36.6 %all_to_all.30 = bf16[16,5,5120]{2,1,0:T(8,128)(2,1)} all-to-all(bf16[16,5,5120]{2,1,0:T(8,128)(2,1)S(1)} %copy.39), channel_id=1, replica_groups=mesh['ctx'=16,'exp'=16] {'exp'}, dimensions={0} | all-to-all | bytes 1638400 | tf_op jit(solution)/shard_map/all_to_all | solution.py:115
  365.0 2.2 reshape.122
  367.2 0.0 all-gather.6.cloned.1.call-update
  367.2 0.2 reduce-scatter.5.cloned.1.call-start
  367.4 139.5 %all-gather.6.cloned.1.call-done = bf16[1280,5120]{1,0:T(8,128)(2,1)} async-done(((bf16[80,5120]{1,0:T(8,128)(2,1)}), bf16[1280,5120]{1,0:T(8,128)(2,1)}) %all-gather.6.cloned.1.call-update) | async-done | bytes 13107216 | tf_op jit(solution)/shard_map/all_gather | solution.py:120
  506.9 10.1 %fusion.8 = f32[1280,256]{1,0:T(8,128)} fusion(bf16[1280,5120]{1,0:T(8,128)(2,1)} %all-gather.6.cloned.1.call-done, bf16[1,5120,256]{2,1,0:T(8,128)(2,1)} %param.21), kind=kOutput, calls=%fused_computation.15 | convolution fusion | flops 3355443200 | bytes 17039360 | tf_op jit(solution)/shard_map/dot_general | solution.py:121
  517.0 20.4 %convolution_convert_fusion = bf16[1280,5120]{1,0:T(8,128)(2,1)} fusion(bf16[1,256,5120]{2,1,0:T(8,128)(2,1)S(1)} %copy-done, bf16[1280,5120]{1,0:T(8,128)(2,1)} %all-gather.6.cloned.1.call-done, bf16[1,5120,256]{2,1,0:T(8,128)(2,1)} %param.22, f32[1280,256]{1,0:T(8,128)} %fusion.8), kind=kOutput, calls=%fused_computation | convolution fusion | flops 6719406080 | bytes 32768000 | tf_op jit(solution)/shard_map/dot_general | solution.py:125
  537.4 0.0 reduce-scatter.5.cloned.1.call-update
  537.4 176.1 %reduce-scatter.5.cloned.1.call-done = bf16[80,5120]{1,0:T(8,128)(2,1)} async-done(((bf16[1280,5120]{1,0:T(8,128)(2,1)}), bf16[80,5120]{1,0:T(8,128)(2,1)}) %reduce-scatter.5.cloned.1.call-update) | async-done | bytes 819216 | tf_op jit(solution)/shard_map/reduce_scatter | solution.py:124
  713.5 2.3 reshape.123
  715.7 37.4 %all_to_all.31 = bf16[16,5,5120]{2,1,0:T(8,128)(2,1)S(1)} all-to-all(bf16[16,5,5120]{2,1,0:T(8,128)(2,1)} %reshape.123), channel_id=1, replica_groups=mesh['ctx'=16,'exp'=16] {'exp'}, dimensions={0} | all-to-all | bytes 1638400 | tf_op jit(solution)/shard_map/all_to_all | solution.py:131
  753.1 1.6 fusion.2
  (28 shorter events, 0.1 us)
Async XLA Ops:
  6.5 510.5 %copy-start = (bf16[1,256,5120]{2,1,0:T(8,128)(2,1)S(1)}, bf16[1,256,5120]{2,1,0:T(8,128)(2,1)}, u32[]{:S(2)}) copy-start(bf16[1,256,5120]{2,1,0:T(8,128)(2,1)} %param.23) | copy-start | bytes 7864324
  6.5 13.7 %copy-start.5 = (bf16[1,64,2560]{2,1,0:T(8,128)(2,1)S(1)}, bf16[1,64,2560]{2,1,0:T(8,128)(2,1)}, u32[]{:S(2)}) copy-start(bf16[1,64,2560]{2,1,0:T(8,128)(2,1)} %param.12) | copy-start | bytes 983044
  6.5 14.1 %copy-start.9 = (s32[1,4]{1,0:T(1,128)S(1)}, s32[1,4]{1,0:T(1,128)}, u32[]{:S(2)}) copy-start(s32[1,4]{1,0:T(1,128)} %param.15) | copy-start | bytes 52
  6.5 65.0 %all-gather.8.cloned.1.call-start = ((), (), s32[]{:S(2)}) async-start(), calls=%async_computation.9 | async-start | bytes 1114112 | tf_op jit(solution)/shard_map/all_gather | solution.py:50
  9.3 64.6 %all-to-all-start = ((bf16[16,64,512]{2,1,0:T(8,128)(2,1)}), bf16[16,64,512]{2,1,0:T(8,128)(2,1)}, u32[]{:S(2)}, u32[]{:S(2)}) async-start(bf16[16,64,512]{2,1,0:T(8,128)(2,1)} %stack.3), calls=%async_computation | async-start | bytes 2097152 | tf_op jit(solution)/shard_map/all_to_all | solution.py:9
  19.5 132.2 %all-gather.10.cloned.1.call-start = ((), (), s32[]{:S(2)}) async-start(), calls=%async_computation.10 | async-start | bytes 2785280 | tf_op jit(solution)/shard_map/all_gather | solution.py:79
  78.5 1.6 copy-start.4
  85.3 70.4 %all-to-all-start.1 = ((bf16[64,16,160]{2,0,1:T(8,128)(2,1)}), bf16[64,16,160]{2,0,1:T(8,128)(2,1)S(1)}, u32[]{:S(2)}, u32[]{:S(2)}) async-start(bf16[64,16,160]{2,0,1:T(8,128)(2,1)} %copy.37), calls=%async_computation.1 | async-start | bytes 1048576 | tf_op jit(solution)/shard_map/all_to_all | solution.py:80
  89.5 234.8 %reduce-scatter.3.cloned.1.call-start = ((), (), s32[]{:S(2)}) async-start(), calls=%async_computation.6 | async-start | bytes 11141120 | tf_op jit(solution)/shard_map/reduce_scatter | solution.py:88
  162.6 0.7 copy-start.7
  162.6 0.9 copy-start.6
  162.6 161.7 %copy-start.1 = (bf16[1,64,5120]{2,1,0:T(8,128)(2,1)S(1)}, bf16[1,64,5120]{2,1,0:T(8,128)(2,1)}, u32[]{:S(2)}) copy-start(bf16[1,64,5120]{2,1,0:T(8,128)(2,1)} %param.16) | copy-start | bytes 1966084
  162.7 163.2 %copy-start.8 = (bf16[5120,16]{0,1:T(8,128)(2,1)S(1)}, bf16[5120,16]{0,1:T(8,128)(2,1)}, u32[]{:S(2)}) copy-start(bf16[5120,16]{0,1:T(8,128)(2,1)} %param.19) | copy-start | bytes 491524
  162.7 344.2 %all-gather.6.cloned.1.call-start = ((), (), s32[]{:S(2)}) async-start(), calls=%async_computation.7 | async-start | bytes 13926400 | tf_op jit(solution)/shard_map/all_gather | solution.py:120
  324.4 3.0 copy-start.2
  367.2 346.3 %reduce-scatter.5.cloned.1.call-start = ((), (), s32[]{:S(2)}) async-start(), calls=%async_computation.8 | async-start | bytes 13926400 | tf_op jit(solution)/shard_map/reduce_scatter | solution.py:124
  715.7 37.4 %copy-start.3 = (bf16[64,5120]{1,0:T(8,128)(2,1)S(1)}, bf16[64,5120]{1,0:T(8,128)(2,1)}, u32[]{:S(2)}) copy-start(bf16[64,5120]{1,0:T(8,128)(2,1)} %reduce-scatter.3.cloned.1.call-done) | copy-start | bytes 1966084
Sparse Core Ops, SparseCore 0:
  10.0 61.4 all-gather.7
  73.3 78.2 all-gather.9
  162.8 161.5 reduce-scatter.2
  367.3 139.5 all-gather.5
  537.5 175.8 reduce-scatter.4
